TPU v7x, 256 devices: a whole 4x4x8 slice. The times are simulated.
256 devices in a mesh: chan: 64 (over z, y_lo, x), ma: 4 (over y_hi, core).
Axes of the slice: x: 4, y: 4 (y_hi: 2, y_lo: 2; y = y_hi * 2 + y_lo), z: 8, core: 2. Of those that a mesh axis runs over, the one named last changes fastest.
Arguments:
- beam_table: bfloat16 [512, 1024, 2048], P(('ma', 'chan')), parts along dimension 0, may hold values from -0.125 to 0.125
- covariance: bfloat16 [8192, 128, 128], P(('ma', 'chan')), parts along dimension 0, as said below
- noise_var: float32 [512, 512], P(('ma', 'chan')), parts along dimension 0, may hold values from 0.5 to 4
- start_field: float32 [512, 512, 256], P(('ma', 'chan')), parts along dimension 0, may hold values from -4 to 4
- probes: float32 [512, 512, 256], P(('ma', 'chan')), parts along dimension 0, may hold values from -6 to 6
Outputs:
- solved: float32 [512, 512, 256], P(('ma', 'chan')), parts along dimension 0
- multipole_band_power: bfloat16 [8192, 128, 128], P(('ma', 'chan')), parts along dimension 0
There are 4 independent parts, one for each index of `ma`. A program takes and returns all parts, laid end to end along the dimension named above; each array names one. Nothing has to cross between parts.
Inputs may be any that keep to these rules, and one draw needn't show every extreme that they name: Each covariance[l] is symmetric with diagonal entries between 1 and 2.
All inputs are finite; a program needn't handle non-finite values.
Results may differ from a plain program's by a relative error of at most 0.009.
Values may be sent and summed in bfloat16 or wider, within the bound.
No kernel may reach another device: no remote copies, remote signals or barrier semaphores. Data moves between devices by JAX's collectives and lax.ppermute only.
A program may use at most 128 MiB of HBM per device.

v0:
```python
import jax
import jax.numpy as jnp
from jax import lax
from jax.sharding import PartitionSpec as P

ITERS = 2
WEIGHT = 0.2


def project_back(beam_table, field_b):
    column_entries = field_b.shape[2] // 2
    reals = field_b[:, :, :column_entries]
    imags = field_b[:, :, column_entries:]
    lower = jnp.concatenate([imags, -reals], axis=2)
    stacked = jnp.concatenate([field_b, lower], axis=1)
    return jnp.einsum("fkl,fkc->flc", beam_table, stacked, preferred_element_type=jnp.float32)


def project_out(beam_table, mixed_back):
    column_entries = mixed_back.shape[2] // 2
    modes = beam_table.shape[1] // 2
    product = jnp.einsum("fkl,flc->fkc", beam_table, mixed_back, preferred_element_type=jnp.float32)
    upper = product[:, :modes]
    lower = product[:, modes:]
    return jnp.concatenate(
        [
            upper[:, :, :column_entries] - lower[:, :, column_entries:],
            upper[:, :, column_entries:] + lower[:, :, :column_entries],
        ],
        axis=2,
    )


def apply_operator(beam_table, covariance, field):
    field_b = field.astype(jnp.bfloat16)
    sky_map = project_back(beam_table, field_b).astype(jnp.bfloat16)
    channel_mixed = jnp.einsum(
        "drj,jdi->rdi",
        covariance,
        lax.all_to_all(sky_map, "chan", split_axis=1, concat_axis=0, tiled=True),
        preferred_element_type=jnp.float32,
    )
    mixed_back = lax.all_to_all(
        channel_mixed.astype(jnp.bfloat16), "chan", split_axis=0, concat_axis=1, tiled=True
    )
    return project_out(beam_table, mixed_back)


def on_device(beam_table, covariance, noise_var, start_field, probes):
    field = start_field
    column_entries = field.shape[2] // 2
    for repeat in range(ITERS):
        image = apply_operator(beam_table, covariance, field)
        field = field + WEIGHT * (probes - image - noise_var[:, :, None] * field)
    final_sky = project_back(beam_table, field.astype(jnp.bfloat16)).astype(jnp.bfloat16)
    collected_parts = lax.all_to_all(final_sky, "chan", split_axis=1, concat_axis=0, tiled=True)
    multipole_band_power = (
        jnp.einsum(
            "mjk,ujk->jmu", collected_parts, collected_parts, preferred_element_type=jnp.float32
        )
        / column_entries
    )
    return (field, multipole_band_power.astype(jnp.bfloat16))


def solution(mesh):
    return jax.shard_map(
        on_device,
        mesh=mesh,
        in_specs=(
            P(("ma", "chan"), None, None),
            P(("ma", "chan"), None, None),
            P(("ma", "chan"), None),
            P(("ma", "chan"), None, None),
            P(("ma", "chan"), None, None),
        ),
        out_specs=(P(("ma", "chan"), None, None), P(("ma", "chan"), None, None)),
        check_vma=False,
    )
```

profile of v0, /device:TPU:2, one launch (start us, length us, event | category | flops | bytes accessed | tf_op | source)
XLA Modules:
  0.0 362.9 jit_solution(1768359897878251081)
XLA Ops:
  0.6 1.6 copy.48
  2.4 7.2 %fusion = bf16[2,2048,256]{1,2,0:T(8,128)(2,1)} fusion(bf16[2,1024,2048]{2,1,0:T(8,128)(2,1)} %param.5, bf16[2,512,128]{1,2,0:T(8,128)(2,1)S(1)} %get-tuple-element.19, bf16[2,512,128]{1,2,0:T(8,128)(2,1)S(1)} %get-tuple-element.18, bf16[2,512,256]{1,2,0:T(8,128)(2,1)S(1)} %convert_element_type.42), kind=kOutput, calls=%fused_computation.3 | convolution fusion | flops 2151677952 | bytes 11534336 | tf_op jit(solution)/shard_map/fkl,fkc->flc/dot_general | solution.py:16
  9.6 6.1 %copy.39 = bf16[2,2048,256]{2,0,1:T(2,128)(2,1)} copy(bf16[2,2048,256]{1,2,0:T(8,128)(2,1)} %fusion) | data formatting | bytes 4194304 | tf_op jit(solution)/shard_map/convert_element_type | solution.py:36
  15.7 63.4 %all_to_all.90 = bf16[2,2048,256]{2,0,1:T(2,128)(2,1)S(1)} all-to-all(bf16[2,2048,256]{2,0,1:T(2,128)(2,1)} %copy.39), channel_id=1, replica_groups=mesh['chan'=64,'ma'=4] {'chan'}, dimensions={1} | all-to-all | bytes 4194304 | tf_op jit(solution)/shard_map/all_to_all | solution.py:40
  79.2 0.3 copy.40
  79.6 3.0 convert_bitcast_fusion.1
  82.6 4.6 %copy.43 = bf16[128,32,256]{2,1,0:T(8,128)(2,1)} copy(bf16[128,32,256]{0,2,1:T(8,128)(2,1)} %convert_bitcast_fusion.1) | data formatting | bytes 4194304 | tf_op jit(solution)/shard_map/convert_element_type | solution.py:44
  87.2 7.1 %all-to-all-start.1 = ((bf16[128,32,256]{2,1,0:T(8,128)(2,1)}), bf16[128,32,256]{2,1,0:T(8,128)(2,1)}, u32[]{:S(2)}, u32[]{:S(2)}) async-start(bf16[128,32,256]{2,1,0:T(8,128)(2,1)} %copy.43), calls=%async_computation.1 | async-start | bytes 4194304 | tf_op jit(solution)/shard_map/all_to_all | solution.py:43
  94.3 1.6 copy.46
  95.8 47.6 %all-to-all-done.1 = bf16[128,32,256]{2,1,0:T(8,128)(2,1)} async-done(((bf16[128,32,256]{2,1,0:T(8,128)(2,1)}), bf16[128,32,256]{2,1,0:T(8,128)(2,1)}, u32[]{:S(2)}, u32[]{:S(2)}) %all-to-all-start.1) | async-done | bytes 2097184 | tf_op jit(solution)/shard_map/all_to_all | solution.py:43
  143.5 1.9 copy.44
  145.4 6.2 %convolution_bitcast_fusion.1 = f32[2,1024,256]{1,2,0:T(8,128)S(1)} fusion(bf16[2,2048,256]{2,1,0:T(8,128)(2,1)S(1)} %bitcast.52, bf16[2,1024,2048]{2,1,0:T(8,128)(2,1)} %param.5), kind=kOutput, calls=%fused_computation.14 | convolution fusion | flops 2147483648 | bytes 12582912 | tf_op jit(solution)/shard_map/fkl,flc->fkc/dot_general | solution.py:22
  151.9 0.4 copy-done.7
  152.3 0.4 fusion.32
  152.8 3.8 %fusion.1 = bf16[2,2048,256]{1,2,0:T(8,128)(2,1)} fusion(bf16[2,1024,2048]{2,1,0:T(8,128)(2,1)S(1)} %bitcast.55, bf16[2,512,128]{1,2,0:T(8,128)(2,1)S(1)} %get-tuple-element.17, bf16[2,512,128]{1,2,0:T(8,128)(2,1)S(1)} %get-tuple-element.16, bf16[2,512,256]{1,2,0:T(8,128)(2,1)S(1)} %fusion.32), kind=kOutput, calls=%fused_computation.4 | convolution fusion | flops 2151677952 | bytes 11534336 | tf_op jit(solution)/shard_map/fkl,fkc->flc/dot_general | solution.py:16
  156.7 6.1 %copy.49 = bf16[2,2048,256]{2,0,1:T(2,128)(2,1)} copy(bf16[2,2048,256]{1,2,0:T(8,128)(2,1)} %fusion.1) | data formatting | bytes 4194304 | tf_op jit(solution)/shard_map/convert_element_type | solution.py:36
  162.8 56.1 %all_to_all.91 = bf16[2,2048,256]{2,0,1:T(2,128)(2,1)S(1)} all-to-all(bf16[2,2048,256]{2,0,1:T(2,128)(2,1)} %copy.49), channel_id=1, replica_groups=mesh['chan'=64,'ma'=4] {'chan'}, dimensions={1} | all-to-all | bytes 4194304 | tf_op jit(solution)/shard_map/all_to_all | solution.py:40
  218.9 0.3 copy.50
  219.3 3.0 convert_bitcast_fusion
  222.3 4.5 %copy.53 = bf16[128,32,256]{2,1,0:T(8,128)(2,1)} copy(bf16[128,32,256]{0,2,1:T(8,128)(2,1)} %convert_bitcast_fusion) | data formatting | bytes 4194304 | tf_op jit(solution)/shard_map/convert_element_type | solution.py:44
  226.9 56.0 %all_to_all.92 = bf16[128,32,256]{2,1,0:T(8,128)(2,1)S(1)} all-to-all(bf16[128,32,256]{2,1,0:T(8,128)(2,1)} %copy.53), channel_id=1, replica_groups=mesh['chan'=64,'ma'=4] {'chan'}, dimensions={0} | all-to-all | bytes 4194304 | tf_op jit(solution)/shard_map/all_to_all | solution.py:43
  283.1 6.2 %convolution_bitcast_fusion = f32[2,1024,256]{1,2,0:T(8,128)S(1)} fusion(bf16[2,2048,256]{2,1,0:T(8,128)(2,1)S(1)} %bitcast.53, bf16[2,1024,2048]{2,1,0:T(8,128)(2,1)} %param.5), kind=kOutput, calls=%fused_computation.13 | convolution fusion | flops 2147483648 | bytes 12582912 | tf_op jit(solution)/shard_map/fkl,flc->fkc/dot_general | solution.py:22
  289.6 0.8 copy-done.3
  290.6 1.5 fusion.36
  292.1 2.5 fusion.2
  294.6 3.8 %copy.57 = bf16[2,2048,256]{2,0,1:T(2,128)(2,1)} copy(bf16[2,2048,256]{1,2,0:T(8,128)(2,1)S(1)} %fusion.2) | data formatting | bytes 4194304 | tf_op jit(solution)/shard_map/convert_element_type | solution.py:55
  298.5 7.0 %all-to-all-start.4 = ((bf16[2,2048,256]{2,0,1:T(2,128)(2,1)}), bf16[2,2048,256]{2,0,1:T(2,128)(2,1)S(1)}, u32[]{:S(2)}, u32[]{:S(2)}) async-start(bf16[2,2048,256]{2,0,1:T(2,128)(2,1)} %copy.57), calls=%async_computation.4 | async-start | bytes 4194304 | tf_op jit(solution)/shard_map/all_to_all | solution.py:56
  305.5 1.3 copy.60
  306.8 47.8 %all-to-all-done.4 = bf16[2,2048,256]{2,0,1:T(2,128)(2,1)S(1)} async-done(((bf16[2,2048,256]{2,0,1:T(2,128)(2,1)}), bf16[2,2048,256]{2,0,1:T(2,128)(2,1)S(1)}, u32[]{:S(2)}, u32[]{:S(2)}) %all-to-all-start.4) | async-done | bytes 2097184 | tf_op jit(solution)/shard_map/all_to_all | solution.py:56
  354.9 3.5 copy.59
  358.4 2.8 all_to_all.84
  361.2 1.7 multiply_convert_fusion
  (34 shorter events, 1.7 us)
Async XLA Ops:
  0.6 79.0 %copy-start = (bf16[32,128,128]{2,1,0:T(8,128)(2,1)S(1)}, bf16[32,128,128]{2,1,0:T(8,128)(2,1)}, u32[]{:S(2)}) copy-start(bf16[32,128,128]{2,1,0:T(8,128)(2,1)} %param.6) | copy-start | bytes 3145732
  87.2 56.3 %all-to-all-start.1 = ((bf16[128,32,256]{2,1,0:T(8,128)(2,1)}), bf16[128,32,256]{2,1,0:T(8,128)(2,1)}, u32[]{:S(2)}, u32[]{:S(2)}) async-start(bf16[128,32,256]{2,1,0:T(8,128)(2,1)} %copy.43), calls=%async_computation.1 | async-start | bytes 4194304 | tf_op jit(solution)/shard_map/all_to_all | solution.py:43
  143.5 9.4 %slice-start = ((s8[8388608]{0:T(1024)(128)(4,1)}), s8[4194304]{0:T(1024)(128)(4,1)S(1)}, s32[]{:S(2)}) async-start(s8[8388608]{0:T(1024)(128)(4,1)} %bitcast.54), calls=%async_computation.5 | async-start | bytes 8388608
  145.4 7.4 %slice-start.1 = ((s8[8388608]{0:T(1024)(128)(4,1)}), s8[4194304]{0:T(1024)(128)(4,1)S(1)}, s32[]{:S(2)}) async-start(s8[8388608]{0:T(1024)(128)(4,1)} %bitcast.54), calls=%async_computation.6 | async-start | bytes 8388608
  151.6 0.7 copy-start.7
  151.9 0.9 copy-start.2
  151.9 1.0 copy-start.4
  282.9 9.2 %slice-start.2 = ((s8[8388608]{0:T(1024)(128)(4,1)}), s8[4194304]{0:T(1024)(128)(4,1)S(1)}, s32[]{:S(2)}) async-start(s8[8388608]{0:T(1024)(128)(4,1)} %bitcast.56), calls=%async_computation.7 | async-start | bytes 8388608
  283.1 9.0 %slice-start.3 = ((s8[8388608]{0:T(1024)(128)(4,1)}), s8[4194304]{0:T(1024)(128)(4,1)S(1)}, s32[]{:S(2)}) async-start(s8[8388608]{0:T(1024)(128)(4,1)} %bitcast.56), calls=%async_computation.8 | async-start | bytes 8388608
  289.4 1.0 copy-start.3
  289.4 1.2 copy-start.5
  298.5 7.0 %copy-start.6 = (f32[2,512,256]{1,2,0:T(8,128)S(1)}, f32[2,512,256]{1,2,0:T(8,128)}, u32[]{:S(2)}) copy-start(f32[2,512,256]{1,2,0:T(8,128)} %get-tuple-element.9) | copy-start | bytes 3145732
  298.5 56.1 %all-to-all-start.4 = ((bf16[2,2048,256]{2,0,1:T(2,128)(2,1)}), bf16[2,2048,256]{2,0,1:T(2,128)(2,1)S(1)}, u32[]{:S(2)}, u32[]{:S(2)}) async-start(bf16[2,2048,256]{2,0,1:T(2,128)(2,1)} %copy.57), calls=%async_computation.4 | async-start | bytes 4194304 | tf_op jit(solution)/shard_map/all_to_all | solution.py:56
  358.4 4.5 %copy-start.1 = (bf16[32,128,128]{2,1,0:T(8,128)(2,1)S(1)}, bf16[32,128,128]{2,1,0:T(8,128)(2,1)}, u32[]{:S(2)}) copy-start(bf16[32,128,128]{2,1,0:T(8,128)(2,1)} %param.6) | copy-start | bytes 3145732
where the time goes:
time: 364 us; the launch traced here: 363 us
  blocking collectives  176 us (48%)
  waiting for transfers between devices  95.4 us (26%)
  local copies, waits for them, and re-layouts  40.8 us (11%)
  matrix products  33.6 us (9%)
  starting transfers between devices  14 us (4%)
    all_to_all x2, blocking collectives, apply_operator(): lax.all_to_all(sky_map, 'chan', split_axis=1, concat_axis=0, tiled=True)  119 us
    all_to_all x1, blocking collectives, apply_operator(): lax.all_to_all(channel_mixed.astype(jnp.bfloat16), 'chan', split_axis=0,...  56 us
    all_to_all x1, waiting for transfers between devices, on_device(): lax.all_to_all(final_sky, 'chan', split_axis=1, concat_axis=0, tiled=True)  47.8 us
    all_to_all x1, waiting for transfers between devices, apply_operator(): lax.all_to_all(channel_mixed.astype(jnp.bfloat16), 'chan', split_axis=0,...  47.6 us
    dot_general x3, matrix products, project_back(): jnp.einsum('fkl,fkc->flc', beam_table, stacked, preferred_element_type=jn...  13.5 us
    dot_general x2, matrix products, project_out(): jnp.einsum('fkl,flc->fkc', beam_table, mixed_back, preferred_element_type...  12.4 us
    convert_element_type x2, local copies, waits for them, and re-layouts, apply_operator(): sky_map = project_back(beam_table, field_b).astype(jnp.bfloat16)  12.2 us
    convert_element_type x2, local copies, waits for them, and re-layouts, apply_operator(): channel_mixed.astype(jnp.bfloat16)  9.14 us
  transfers between devices with their start and end apart: 2, of which 2 were waited for; matrix products, arithmetic and copies ran while one was open for 1% of the time, Pallas kernels for 0%

commit v1 on v0

--- a/solution.py
+++ b/solution.py
@@ -53,7 +53,9 @@
         image = apply_operator(beam_table, covariance, field)
         field = field + WEIGHT * (probes - image - noise_var[:, :, None] * field)
     final_sky = project_back(beam_table, field.astype(jnp.bfloat16)).astype(jnp.bfloat16)
-    collected_parts = lax.all_to_all(final_sky, "chan", split_axis=1, concat_axis=0, tiled=True)
+    collected_parts = jnp.concatenate(
+        lax.all_to_all(jnp.stack(jnp.split(final_sky, lax.axis_size("chan"), 1)), "chan", 0, 0), 0
+    )
     multipole_band_power = (
         jnp.einsum(
             "mjk,ujk->jmu", collected_parts, collected_parts, preferred_element_type=jnp.float32

time: 364 us -> 467 us (1.28)
  local copies, waits for them, and re-layouts: 40.8 us -> 140 us
    another operation x0 -> x69, local copies, waits for them, and re-layouts: none -> 60.4 us  [on_device(): jnp.stack(jnp.split(final_sky, lax.axis_size('chan'), 1))]
    unnamed x27 -> x150, local copies, waits for them, and re-layouts: 6.02 us -> 54.9 us
    all_to_all x3 -> x0, local copies, waits for them, and re-layouts: 6.6 us -> none  [on_device(): lax.all_to_all(final_sky, 'chan', split_axis=1, concat_axis=0, tiled=True)]
where the time goes in v1:
time: 467 us; the launch traced here: 464 us
  blocking collectives  175 us (37%)
  local copies, waits for them, and re-layouts  140 us (30%)
  waiting for transfers between devices  95.4 us (20%)
  matrix products  35.4 us (8%)
  starting transfers between devices  14.3 us (3%)
    all_to_all x2, blocking collectives, apply_operator(): lax.all_to_all(sky_map, 'chan', split_axis=1, concat_axis=0, tiled=True)  119 us
    another operation x69, local copies, waits for them, and re-layouts, on_device(): jnp.stack(jnp.split(final_sky, lax.axis_size('chan'), 1))  60.4 us
    all_to_all x1, blocking collectives, apply_operator(): lax.all_to_all(channel_mixed.astype(jnp.bfloat16), 'chan', split_axis=0,...  56 us
    unnamed x150, local copies, waits for them, and re-layouts  54.9 us
    all_to_all x1, waiting for transfers between devices, on_device(): lax.all_to_all(jnp.stack(jnp.split(final_sky, lax.axis_size('chan'), 1)),...  47.8 us
    all_to_all x1, waiting for transfers between devices, apply_operator(): lax.all_to_all(channel_mixed.astype(jnp.bfloat16), 'chan', split_axis=0,...  47.6 us
    dot_general x3, matrix products, project_back(): jnp.einsum('fkl,fkc->flc', beam_table, stacked, preferred_element_type=jn...  13.5 us
    dot_general x2, matrix products, project_out(): jnp.einsum('fkl,flc->fkc', beam_table, mixed_back, preferred_element_type...  12.4 us
  transfers between devices with their start and end apart: 2, of which 2 were waited for; matrix products, arithmetic and copies ran while one was open for 1% of the time, Pallas kernels for 0%

profile of v1, /device:TPU:2, one launch (start us, length us, event | category | flops | bytes accessed | tf_op | source)
XLA Modules:
  0.0 464.3 jit_solution(5602822884990466275)
XLA Ops:
  0.6 1.6 copy.49
  2.4 7.2 %fusion = bf16[2,2048,256]{1,2,0:T(8,128)(2,1)} fusion(bf16[2,1024,2048]{2,1,0:T(8,128)(2,1)} %param.5, bf16[2,512,128]{1,2,0:T(8,128)(2,1)S(1)} %get-tuple-element.83, bf16[2,512,128]{1,2,0:T(8,128)(2,1)S(1)} %get-tuple-element.82, bf16[2,512,256]{1,2,0:T(8,128)(2,1)S(1)} %convert_element_type.42), kind=kOutput, calls=%fused_computation.3 | convolution fusion | flops 2151677952 | bytes 11534336 | tf_op jit(solution)/shard_map/fkl,fkc->flc/dot_general | solution.py:16
  9.6 6.2 %copy.40 = bf16[2,2048,256]{2,0,1:T(2,128)(2,1)} copy(bf16[2,2048,256]{1,2,0:T(8,128)(2,1)} %fusion) | data formatting | bytes 4194304 | tf_op jit(solution)/shard_map/convert_element_type | solution.py:36
  15.8 63.4 %all_to_all.77 = bf16[2,2048,256]{2,0,1:T(2,128)(2,1)S(1)} all-to-all(bf16[2,2048,256]{2,0,1:T(2,128)(2,1)} %copy.40), channel_id=1, replica_groups=mesh['chan'=64,'ma'=4] {'chan'}, dimensions={1} | all-to-all | bytes 4194304 | tf_op jit(solution)/shard_map/all_to_all | solution.py:40
  79.7 3.0 convert_bitcast_fusion.1
  82.7 4.6 copy.44
  87.3 7.1 %all-to-all-start.1 = ((bf16[128,32,256]{2,1,0:T(8,128)(2,1)}), bf16[128,32,256]{2,1,0:T(8,128)(2,1)}, u32[]{:S(2)}, u32[]{:S(2)}) async-start(bf16[128,32,256]{2,1,0:T(8,128)(2,1)} %copy.44), calls=%async_computation.1 | async-start | bytes 4194304 | tf_op jit(solution)/shard_map/all_to_all | solution.py:43
  95.9 47.6 %all-to-all-done.1 = bf16[128,32,256]{2,1,0:T(8,128)(2,1)} async-done(((bf16[128,32,256]{2,1,0:T(8,128)(2,1)}), bf16[128,32,256]{2,1,0:T(8,128)(2,1)}, u32[]{:S(2)}, u32[]{:S(2)}) %all-to-all-start.1) | async-done | bytes 2097184 | tf_op jit(solution)/shard_map/all_to_all | solution.py:43
  143.6 1.9 copy.45
  145.5 6.2 %convolution_bitcast_fusion.1 = f32[2,1024,256]{1,2,0:T(8,128)S(1)} fusion(bf16[2,2048,256]{2,1,0:T(8,128)(2,1)S(1)} %bitcast.174, bf16[2,1024,2048]{2,1,0:T(8,128)(2,1)} %param.5), kind=kOutput, calls=%fused_computation.16 | convolution fusion | flops 2147483648 | bytes 12582912 | tf_op jit(solution)/shard_map/fkl,flc->fkc/dot_general | solution.py:22
  152.9 3.8 fusion.1
  156.8 6.2 %copy.50 = bf16[2,2048,256]{2,0,1:T(2,128)(2,1)} copy(bf16[2,2048,256]{1,2,0:T(8,128)(2,1)} %fusion.1) | data formatting | bytes 4194304 | tf_op jit(solution)/shard_map/convert_element_type | solution.py:36
  162.9 56.1 %all_to_all.78 = bf16[2,2048,256]{2,0,1:T(2,128)(2,1)S(1)} all-to-all(bf16[2,2048,256]{2,0,1:T(2,128)(2,1)} %copy.50), channel_id=1, replica_groups=mesh['chan'=64,'ma'=4] {'chan'}, dimensions={1} | all-to-all | bytes 4194304 | tf_op jit(solution)/shard_map/all_to_all | solution.py:40
  219.5 3.0 convert_bitcast_fusion
  222.5 4.6 copy.54
  227.1 56.0 %all_to_all.79 = bf16[128,32,256]{2,1,0:T(8,128)(2,1)S(1)} all-to-all(bf16[128,32,256]{2,1,0:T(8,128)(2,1)} %copy.54), channel_id=1, replica_groups=mesh['chan'=64,'ma'=4] {'chan'}, dimensions={0} | all-to-all | bytes 4194304 | tf_op jit(solution)/shard_map/all_to_all | solution.py:43
  283.3 6.2 %convolution_bitcast_fusion = f32[2,1024,256]{1,2,0:T(8,128)S(1)} fusion(bf16[2,2048,256]{2,1,0:T(8,128)(2,1)S(1)} %bitcast.175, bf16[2,1024,2048]{2,1,0:T(8,128)(2,1)} %param.5), kind=kOutput, calls=%fused_computation.15 | convolution fusion | flops 2147483648 | bytes 12582912 | tf_op jit(solution)/shard_map/fkl,flc->fkc/dot_general | solution.py:22
  292.3 2.4 fusion.2
  295.0 2.0 slice_bitcast_fusion.38
  297.0 2.0 slice_bitcast_fusion
  312.5 1.6 copy.78
  314.1 1.6 copy.77
  315.7 1.6 copy.76
  317.4 1.6 copy.75
  319.0 1.6 copy.74
  320.6 1.6 copy.73
  322.2 1.6 copy.72
  328.6 1.6 copy.68
  333.4 1.6 copy.65
  404.5 7.2 %all-to-all-start.4 = ((bf16[64,2,32,256]{3,2,1,0:T(8,128)(2,1)}), bf16[64,2,32,256]{3,2,1,0:T(8,128)(2,1)S(1)}, u32[]{:S(2)}, u32[]{:S(2)}) async-start(bf16[64,2,32,256]{3,2,1,0:T(8,128)(2,1)} %constant_dynamic-update-slice_fusion), calls=%async_computation.4 | async-start | bytes 4194304 | tf_op jit(solution)/shard_map/all_to_all | solution.py:57
  413.1 47.8 %all-to-all-done.4 = bf16[64,2,32,256]{3,2,1,0:T(8,128)(2,1)S(1)} async-done(((bf16[64,2,32,256]{3,2,1,0:T(8,128)(2,1)}), bf16[64,2,32,256]{3,2,1,0:T(8,128)(2,1)S(1)}, u32[]{:S(2)}, u32[]{:S(2)}) %all-to-all-start.4) | async-done | bytes 2097184 | tf_op jit(solution)/shard_map/all_to_all | solution.py:57
  460.9 3.4 multiply_convert_fusion
  (222 shorter events, 98.6 us)
Async XLA Ops:
  0.6 79.0 %copy-start = (bf16[32,128,128]{2,1,0:T(8,128)(2,1)S(1)}, bf16[32,128,128]{2,1,0:T(8,128)(2,1)}, u32[]{:S(2)}) copy-start(bf16[32,128,128]{2,1,0:T(8,128)(2,1)} %param.6) | copy-start | bytes 3145732
  87.3 56.2 %all-to-all-start.1 = ((bf16[128,32,256]{2,1,0:T(8,128)(2,1)}), bf16[128,32,256]{2,1,0:T(8,128)(2,1)}, u32[]{:S(2)}, u32[]{:S(2)}) async-start(bf16[128,32,256]{2,1,0:T(8,128)(2,1)} %copy.44), calls=%async_computation.1 | async-start | bytes 4194304 | tf_op jit(solution)/shard_map/all_to_all | solution.py:43
  312.5 39.9 %copy-start.13 = (bf16[1,2,32,256]{2,3,1,0:T(8,128)(2,1)S(1)}, bf16[1,2,32,256]{2,3,1,0:T(8,128)(2,1)}, u32[]{:S(2)}) copy-start(bf16[1,2,32,256]{2,3,1,0:T(8,128)(2,1)} %get-tuple-element.21) | copy-start | bytes 98308
  314.1 39.0 %copy-start.12 = (bf16[1,2,32,256]{2,3,1,0:T(8,128)(2,1)S(1)}, bf16[1,2,32,256]{2,3,1,0:T(8,128)(2,1)}, u32[]{:S(2)}) copy-start(bf16[1,2,32,256]{2,3,1,0:T(8,128)(2,1)} %get-tuple-element.22) | copy-start | bytes 98308
  315.7 37.4 %copy-start.11 = (bf16[1,2,32,256]{2,3,1,0:T(8,128)(2,1)S(1)}, bf16[1,2,32,256]{2,3,1,0:T(8,128)(2,1)}, u32[]{:S(2)}) copy-start(bf16[1,2,32,256]{2,3,1,0:T(8,128)(2,1)} %get-tuple-element.23) | copy-start | bytes 98308
  317.4 35.9 %copy-start.10 = (bf16[1,2,32,256]{2,3,1,0:T(8,128)(2,1)S(1)}, bf16[1,2,32,256]{2,3,1,0:T(8,128)(2,1)}, u32[]{:S(2)}) copy-start(bf16[1,2,32,256]{2,3,1,0:T(8,128)(2,1)} %get-tuple-element.24) | copy-start | bytes 98308
  319.0 34.4 %copy-start.9 = (bf16[1,2,32,256]{2,3,1,0:T(8,128)(2,1)S(1)}, bf16[1,2,32,256]{2,3,1,0:T(8,128)(2,1)}, u32[]{:S(2)}) copy-start(bf16[1,2,32,256]{2,3,1,0:T(8,128)(2,1)} %get-tuple-element.25) | copy-start | bytes 98308
  320.6 32.9 %copy-start.8 = (bf16[1,2,32,256]{2,3,1,0:T(8,128)(2,1)S(1)}, bf16[1,2,32,256]{2,3,1,0:T(8,128)(2,1)}, u32[]{:S(2)}) copy-start(bf16[1,2,32,256]{2,3,1,0:T(8,128)(2,1)} %get-tuple-element.26) | copy-start | bytes 98308
  322.2 31.3 %copy-start.7 = (bf16[1,2,32,256]{2,3,1,0:T(8,128)(2,1)S(1)}, bf16[1,2,32,256]{2,3,1,0:T(8,128)(2,1)}, u32[]{:S(2)}) copy-start(bf16[1,2,32,256]{2,3,1,0:T(8,128)(2,1)} %get-tuple-element.27) | copy-start | bytes 98308
  353.8 21.6 %copy-start.35 = (bf16[1,2,32,256]{3,2,1,0:T(8,128)(2,1)S(1)}, bf16[1,2,32,256]{3,2,1,0:T(8,128)(2,1)}, u32[]{:S(2)}) copy-start(bf16[1,2,32,256]{3,2,1,0:T(8,128)(2,1)} %copy.74) | copy-start | bytes 98308
  353.8 22.2 %copy-start.34 = (bf16[1,2,32,256]{3,2,1,0:T(8,128)(2,1)S(1)}, bf16[1,2,32,256]{3,2,1,0:T(8,128)(2,1)}, u32[]{:S(2)}) copy-start(bf16[1,2,32,256]{3,2,1,0:T(8,128)(2,1)} %copy.75) | copy-start | bytes 98308
  353.8 22.8 %copy-start.33 = (bf16[1,2,32,256]{3,2,1,0:T(8,128)(2,1)S(1)}, bf16[1,2,32,256]{3,2,1,0:T(8,128)(2,1)}, u32[]{:S(2)}) copy-start(bf16[1,2,32,256]{3,2,1,0:T(8,128)(2,1)} %copy.76) | copy-start | bytes 98308
  353.9 23.3 %copy-start.32 = (bf16[1,2,32,256]{3,2,1,0:T(8,128)(2,1)S(1)}, bf16[1,2,32,256]{3,2,1,0:T(8,128)(2,1)}, u32[]{:S(2)}) copy-start(bf16[1,2,32,256]{3,2,1,0:T(8,128)(2,1)} %copy.77) | copy-start | bytes 98308
  353.9 23.9 %copy-start.31 = (bf16[1,2,32,256]{3,2,1,0:T(8,128)(2,1)S(1)}, bf16[1,2,32,256]{3,2,1,0:T(8,128)(2,1)}, u32[]{:S(2)}) copy-start(bf16[1,2,32,256]{3,2,1,0:T(8,128)(2,1)} %copy.78) | copy-start | bytes 98308
  354.0 24.4 %copy-start.30 = (bf16[1,2,32,256]{3,2,1,0:T(8,128)(2,1)S(1)}, bf16[1,2,32,256]{3,2,1,0:T(8,128)(2,1)}, u32[]{:S(2)}) copy-start(bf16[1,2,32,256]{3,2,1,0:T(8,128)(2,1)} %copy.79) | copy-start | bytes 98308
  354.0 25.0 %copy-start.29 = (bf16[1,2,32,256]{3,2,1,0:T(8,128)(2,1)S(1)}, bf16[1,2,32,256]{3,2,1,0:T(8,128)(2,1)}, u32[]{:S(2)}) copy-start(bf16[1,2,32,256]{3,2,1,0:T(8,128)(2,1)} %copy.80) | copy-start | bytes 98308
  354.0 25.6 %copy-start.28 = (bf16[1,2,32,256]{3,2,1,0:T(8,128)(2,1)S(1)}, bf16[1,2,32,256]{3,2,1,0:T(8,128)(2,1)}, u32[]{:S(2)}) copy-start(bf16[1,2,32,256]{3,2,1,0:T(8,128)(2,1)} %copy.81) | copy-start | bytes 98308
  354.1 26.1 %copy-start.27 = (bf16[1,2,32,256]{3,2,1,0:T(8,128)(2,1)S(1)}, bf16[1,2,32,256]{3,2,1,0:T(8,128)(2,1)}, u32[]{:S(2)}) copy-start(bf16[1,2,32,256]{3,2,1,0:T(8,128)(2,1)} %copy.82) | copy-start | bytes 98308
  354.1 26.7 %copy-start.26 = (bf16[1,2,32,256]{3,2,1,0:T(8,128)(2,1)S(1)}, bf16[1,2,32,256]{3,2,1,0:T(8,128)(2,1)}, u32[]{:S(2)}) copy-start(bf16[1,2,32,256]{3,2,1,0:T(8,128)(2,1)} %copy.83) | copy-start | bytes 98308
  355.1 42.1 %copy-start.25 = (bf16[1,2,32,256]{3,2,1,0:T(8,128)(2,1)S(1)}, bf16[1,2,32,256]{3,2,1,0:T(8,128)(2,1)}, u32[]{:S(2)}) copy-start(bf16[1,2,32,256]{3,2,1,0:T(8,128)(2,1)} %copy.110) | copy-start | bytes 98308
  355.2 42.6 %copy-start.24 = (bf16[1,2,32,256]{3,2,1,0:T(8,128)(2,1)S(1)}, bf16[1,2,32,256]{3,2,1,0:T(8,128)(2,1)}, u32[]{:S(2)}) copy-start(bf16[1,2,32,256]{3,2,1,0:T(8,128)(2,1)} %copy.111) | copy-start | bytes 98308
  355.3 43.2 %copy-start.23 = (bf16[1,2,32,256]{3,2,1,0:T(8,128)(2,1)S(1)}, bf16[1,2,32,256]{3,2,1,0:T(8,128)(2,1)}, u32[]{:S(2)}) copy-start(bf16[1,2,32,256]{3,2,1,0:T(8,128)(2,1)} %copy.112) | copy-start | bytes 98308
  355.3 43.8 %copy-start.22 = (bf16[1,2,32,256]{3,2,1,0:T(8,128)(2,1)S(1)}, bf16[1,2,32,256]{3,2,1,0:T(8,128)(2,1)}, u32[]{:S(2)}) copy-start(bf16[1,2,32,256]{3,2,1,0:T(8,128)(2,1)} %copy.113) | copy-start | bytes 98308
  355.3 44.4 %copy-start.21 = (bf16[1,2,32,256]{3,2,1,0:T(8,128)(2,1)S(1)}, bf16[1,2,32,256]{3,2,1,0:T(8,128)(2,1)}, u32[]{:S(2)}) copy-start(bf16[1,2,32,256]{3,2,1,0:T(8,128)(2,1)} %copy.114) | copy-start | bytes 98308
  355.4 44.9 %copy-start.20 = (bf16[1,2,32,256]{3,2,1,0:T(8,128)(2,1)S(1)}, bf16[1,2,32,256]{3,2,1,0:T(8,128)(2,1)}, u32[]{:S(2)}) copy-start(bf16[1,2,32,256]{3,2,1,0:T(8,128)(2,1)} %copy.115) | copy-start | bytes 98308
  355.4 45.5 %copy-start.19 = (bf16[1,2,32,256]{3,2,1,0:T(8,128)(2,1)S(1)}, bf16[1,2,32,256]{3,2,1,0:T(8,128)(2,1)}, u32[]{:S(2)}) copy-start(bf16[1,2,32,256]{3,2,1,0:T(8,128)(2,1)} %copy.116) | copy-start | bytes 98308
  355.5 46.0 %copy-start.18 = (bf16[1,2,32,256]{3,2,1,0:T(8,128)(2,1)S(1)}, bf16[1,2,32,256]{3,2,1,0:T(8,128)(2,1)}, u32[]{:S(2)}) copy-start(bf16[1,2,32,256]{3,2,1,0:T(8,128)(2,1)} %copy.117) | copy-start | bytes 98308
  355.5 46.6 %copy-start.17 = (bf16[1,2,32,256]{3,2,1,0:T(8,128)(2,1)S(1)}, bf16[1,2,32,256]{3,2,1,0:T(8,128)(2,1)}, u32[]{:S(2)}) copy-start(bf16[1,2,32,256]{3,2,1,0:T(8,128)(2,1)} %copy.118) | copy-start | bytes 98308
  355.5 47.2 %copy-start.16 = (bf16[1,2,32,256]{3,2,1,0:T(8,128)(2,1)S(1)}, bf16[1,2,32,256]{3,2,1,0:T(8,128)(2,1)}, u32[]{:S(2)}) copy-start(bf16[1,2,32,256]{3,2,1,0:T(8,128)(2,1)} %copy.119) | copy-start | bytes 98308
  355.6 47.7 %copy-start.15 = (bf16[1,2,32,256]{3,2,1,0:T(8,128)(2,1)S(1)}, bf16[1,2,32,256]{3,2,1,0:T(8,128)(2,1)}, u32[]{:S(2)}) copy-start(bf16[1,2,32,256]{3,2,1,0:T(8,128)(2,1)} %copy.120) | copy-start | bytes 98308
  355.6 48.3 %copy-start.14 = (bf16[1,2,32,256]{3,2,1,0:T(8,128)(2,1)S(1)}, bf16[1,2,32,256]{3,2,1,0:T(8,128)(2,1)}, u32[]{:S(2)}) copy-start(bf16[1,2,32,256]{3,2,1,0:T(8,128)(2,1)} %copy.121) | copy-start | bytes 98308
  404.5 56.4 %all-to-all-start.4 = ((bf16[64,2,32,256]{3,2,1,0:T(8,128)(2,1)}), bf16[64,2,32,256]{3,2,1,0:T(8,128)(2,1)S(1)}, u32[]{:S(2)}, u32[]{:S(2)}) async-start(bf16[64,2,32,256]{3,2,1,0:T(8,128)(2,1)} %constant_dynamic-update-slice_fusion), calls=%async_computation.4 | async-start | bytes 4194304 | tf_op jit(solution)/shard_map/all_to_all | solution.py:57
  (12 other events, 71.5 us)
